TPU v7x, 256 devices: a whole 4x4x8 slice. The times are simulated.
256 devices in a mesh: wide: 64 (over x, z, core), narrow: 4 (over y).
Axes of the slice: x: 4, y: 4, z: 8, core: 2. Of those that a mesh axis runs over, the one named last changes fastest.
Arguments:
- attn_heads: bfloat16 [8192, 1536], P('wide', 'narrow'), may hold values from -6 to 6
- w_out: bfloat16 [1536, 1536], P('narrow'), may hold values from -0.21875 to 0.21875
- residual: bfloat16 [8192, 1536], P('wide', 'narrow'), may hold values from -6 to 6
- norm_gain: float32 [1536], replicated, may hold values from 0.1 to 1.9
- route_ids: int32 [8192, 4], P('wide'), may hold values from 0 to 31, all different within a row; in each aligned block of 128 rows (0 to 127, 128 to 255, ...) at most 32 rows name the same one
- route_weight: float32 [8192, 4], P('wide'), may hold values from 0.1 to 1
- row_order: int32 [8192], P('wide'), may hold values from 0 to 8191, as said below
- slot_expert: int32 [64], replicated, may hold values from 0 to 31, as said below
- w_in: bfloat16 [64, 2, 768, 1536], P('wide', None, 'narrow')
- w_down: bfloat16 [64, 768, 1536], P('wide', 'narrow')
Outputs:
- block_out: bfloat16 [8192, 1536], P('wide', 'narrow')
Inputs may be any that keep to these rules, and one draw needn't show every extreme that they name: `route_ids`: each row names 4 different experts; among the 128 rows of one index of wide no expert is named more than 32 times. `row_order`: A permutation of the rows; of the 128 rows of each index of wide, exactly 2 have their initial position among the rows of each index of wide. `slot_expert`: every expert is held by one or more slots; slots holding the same expert hold equal w_in and w_down.
All inputs are finite; a program needn't handle non-finite values.
Results may differ from a plain program's by a relative error of at most 0.017.
Values may be sent and summed in bfloat16 or wider, within the bound.
No kernel may reach another device: no remote copies, remote signals or barrier semaphores. Data moves between devices by JAX's collectives and lax.ppermute only.
A program may use at most 128 MiB of HBM per device.

v0:
```python
import jax
import jax.numpy as jnp
from jax import lax
from jax.sharding import PartitionSpec as P

EXPERTS = 32
CAP = 32


def running_rank(onehot):
    return jnp.sum((jnp.cumsum(onehot, axis=0) - onehot) * onehot, axis=1)


def local(
    attn_heads,
    w_out,
    residual,
    norm_gain,
    route_ids,
    route_weight,
    row_order,
    slot_expert,
    w_in,
    w_down,
):
    row_count = residual.shape[0]
    wide_count = lax.axis_size("wide")
    narrow_count = lax.axis_size("narrow")
    width_local = residual.shape[1]
    model_width = width_local * narrow_count
    me_narrow = lax.axis_index("narrow")
    slot_local = w_in.shape[0]
    hid_local = w_down.shape[1]
    both = jnp.concatenate([w_in.reshape(slot_local, 2 * hid_local, model_width), w_down], axis=1)
    both = lax.all_gather(both, "narrow", axis=0, tiled=False)
    w_in_all = both[:, :, : 2 * hid_local].reshape(
        narrow_count, slot_local, 2, hid_local, model_width
    )
    w_down_all = both[:, :, 2 * hid_local :]
    partial_terms = jnp.dot(attn_heads, w_out, preferred_element_type=jnp.float32)
    projected = lax.psum_scatter(
        partial_terms.astype(jnp.bfloat16), "narrow", scatter_dimension=1, tiled=True
    ).astype(jnp.float32)
    hidden = (residual.astype(jnp.float32) + projected).astype(jnp.bfloat16)
    hidden_f = hidden.astype(jnp.float32)
    whole_rows = lax.all_gather(hidden, "narrow", axis=1, tiled=True).astype(jnp.float32)
    mean_sq = jnp.mean(whole_rows * whole_rows, axis=1, keepdims=True)
    normed = (whole_rows * lax.rsqrt(mean_sq + 1e-06) * norm_gain).astype(jnp.bfloat16)
    slot_count = slot_expert.shape[0]
    top_count = route_ids.shape[1]
    band = CAP // narrow_count
    held = (slot_expert[None, :] == jnp.arange(EXPERTS, dtype=jnp.int32)[:, None]).astype(jnp.int32)
    copies = jnp.sum(held, axis=1)
    replica_rank = jnp.cumsum(held, axis=1) - held
    flat_ids = route_ids.reshape(-1)
    choose_expert = (flat_ids[:, None] == jnp.arange(EXPERTS, dtype=jnp.int32)[None, :]).astype(
        jnp.int32
    )
    copy_count = jnp.sum(choose_expert * copies[None, :], axis=1)
    replica = jnp.repeat(row_order, top_count) % copy_count
    held_rows = jnp.sum(choose_expert[:, :, None] * held[None, :, :], axis=1)
    rank_rows = jnp.sum(choose_expert[:, :, None] * replica_rank[None, :, :], axis=1)
    slot_hit = held_rows * (rank_rows == replica[:, None]).astype(jnp.int32)
    slot_index = jnp.sum(slot_hit * jnp.arange(slot_count, dtype=jnp.int32)[None, :], axis=1)
    rank = running_rank(slot_hit)
    position = slot_index * CAP + rank
    send_at = jnp.where(
        rank // band == me_narrow, slot_index * band + rank % band, slot_count * band
    )
    outgoing = (
        jnp.zeros((slot_count * band, model_width), jnp.bfloat16)
        .at[send_at]
        .set(jnp.repeat(normed, top_count, axis=0), mode="drop")
    )
    outgoing = outgoing.reshape(wide_count, slot_local, band, model_width)
    arrived = lax.all_to_all(outgoing, "wide", split_axis=0, concat_axis=0, tiled=True)
    gate_up = jnp.einsum(
        "nscd,qsghd->nscgqh", arrived, w_in_all, preferred_element_type=jnp.float32
    )
    active = (jax.nn.relu(gate_up[:, :, :, 0]) * gate_up[:, :, :, 1]).astype(jnp.bfloat16)
    lowered = jnp.einsum(
        "nscqh,qshd->qnscd", active, w_down_all, preferred_element_type=jnp.float32
    )
    pieces = lowered.astype(jnp.bfloat16).astype(jnp.float32)
    summed = jnp.sum(pieces, axis=0).astype(jnp.bfloat16)
    summed = summed.reshape(wide_count, slot_local, band, narrow_count, width_local)
    summed = lax.all_to_all(summed, "narrow", split_axis=3, concat_axis=2, tiled=True)
    summed = summed.reshape(wide_count, slot_local, CAP, width_local)
    returned = lax.all_to_all(summed, "wide", split_axis=0, concat_axis=0, tiled=True)
    expert_out = returned.reshape(slot_count * CAP, width_local)[position]
    weighted = route_weight[:, :, None] * expert_out.reshape(
        row_count, top_count, width_local
    ).astype(jnp.float32)
    mixed = (hidden_f + jnp.sum(weighted, axis=1)).astype(jnp.bfloat16)
    pair_rows = row_count // wide_count
    target_dev = row_order // row_count
    target_place = row_order % row_count
    choose_target = (
        target_dev[:, None] == jnp.arange(wide_count, dtype=jnp.int32)[None, :]
    ).astype(jnp.int32)
    packed_index = target_dev * pair_rows + running_rank(choose_target)
    packed = jnp.zeros((row_count, width_local), jnp.bfloat16).at[packed_index].set(mixed)
    places = jnp.zeros((row_count,), jnp.int32).at[packed_index].set(target_place)
    assert row_count <= 256 and pair_rows <= width_local
    place_row = jnp.zeros((wide_count, 1, width_local), jnp.bfloat16)
    place_row = place_row.at[:, 0, :pair_rows].set(
        places.reshape(wide_count, pair_rows).astype(jnp.bfloat16)
    )
    packed = jnp.concatenate(
        [packed.reshape(wide_count, pair_rows, width_local), place_row], axis=1
    )
    arrived_all = lax.all_to_all(packed, "wide", split_axis=0, concat_axis=0, tiled=True)
    arrived_rows = arrived_all[:, :pair_rows]
    arrived_places = arrived_all[:, pair_rows, :pair_rows].astype(jnp.int32)
    return (
        jnp.zeros((row_count, width_local), jnp.bfloat16)
        .at[arrived_places.reshape(-1)]
        .set(arrived_rows.reshape(row_count, width_local))
    )


def solution(mesh):
    placed = (
        P("wide", "narrow"),
        P("narrow", None),
        P("wide", "narrow"),
        P(),
        P("wide", None),
        P("wide", None),
        P("wide"),
        P(),
        P("wide", None, "narrow", None),
        P("wide", "narrow", None),
    )
    return jax.shard_map(
        local, mesh=mesh, in_specs=placed, out_specs=P("wide", "narrow"), check_vma=False
    )
```

profile of v0, /device:TPU:1, one launch (start us, length us, event | category | flops | bytes accessed | tf_op | source)
XLA Modules:
  0.0 238.9 jit_solution(3613635565145867335)
XLA Ops:
  6.5 1.3 copy-done
  7.8 1.3 convolution_convert_fusion
  9.1 1.0 copy.54
  10.1 1.4 pad_maximum_fusion
  11.6 0.6 copy-done.6
  12.7 0.2 reduce_window_sum.38
  13.1 0.9 multiply_reduce_fusion.1
  14.2 1.2 reduce-window.6
  15.4 0.2 slice_reduce_fusion
  15.9 19.5 %reduce-scatter.4.cloned.1.call-done = bf16[384,128]{1,0:T(8,128)(2,1)} async-done(((bf16[1536,128]{1,0:T(8,128)(2,1)}), bf16[384,128]{1,0:T(8,128)(2,1)}) %reduce-scatter.4.cloned.1.call-update) | async-done | bytes 98320
  35.4 1.0 copy.55
  36.4 10.2 %all_gather.11 = bf16[128,1536]{1,0:T(8,128)(2,1)S(1)} all-gather(bf16[128,384]{1,0:T(8,128)(2,1)S(1)} %add_convert_fusion.1), channel_id=1, replica_groups=mesh['wide'=64,'narrow'=4] {'narrow'}, dimensions={1}, use_global_device_ids=true | all-gather | bytes 491520 | tf_op jit(solution)/shard_map/all_gather | solution.py:46
  47.0 0.4 broadcast_in_dim.24
  47.4 1.4 reshape.402
  48.8 5.2 %scatter_custom_fusion = bf16[512,1536]{1,0:T(8,128)(2,1)} fusion(s32[512]{0:T(512)S(1)} %bitcast.85, bf16[512,1536]{1,0:T(8,128)(2,1)} %reshape.402, bf16[]{:T(256)} %constant.111.clone.1), kind=kCustom, calls=%fused_computation.26 | custom fusion | bytes 1573376 | tf_op jit(solution)/shard_map/scatter | solution.py:73
  54.0 15.6 %all-to-all-start = ((bf16[64,1,8,1536]{3,2,1,0:T(8,128)(2,1)}), bf16[64,1,8,1536]{3,2,1,0:T(8,128)(2,1)S(1)}, u32[]{:S(2)}, u32[]{:S(2)}) async-start(bf16[64,1,8,1536]{3,2,1,0:T(8,128)(2,1)} %bitcast.14), calls=%async_computation | async-start | bytes 3145728 | tf_op jit(solution)/shard_map/all_to_all | solution.py:76
  69.6 44.3 %all-gather.3.cloned.1.call-done = bf16[4,576,1536]{2,1,0:T(8,128)(2,1)} async-done(((bf16[1,576,1536]{2,1,0:T(8,128)(2,1)}), bf16[4,576,1536]{2,1,0:T(8,128)(2,1)}) %all-gather.3.cloned.1.call-update) | async-done | bytes 7077904 | tf_op jit(solution)/shard_map/all_gather | solution.py:35
  114.0 4.9 %slice.58 = bf16[4,1,384,1536]{3,2,0,1:T(8,128)(2,1)} slice(bf16[4,1,576,1536]{3,2,0,1:T(8,128)(2,1)} %bitcast.75), slice={[0:4], [0:1], [0:384], [0:1536]} | slice | bytes 9437184 | tf_op jit(solution)/shard_map/slice | solution.py:36
  118.8 5.3 %convolution_bitcast_fusion = f32[64,1,8,2,4,192]{5,0,2,3,4,1:T(8,128)S(1)} fusion(bf16[4,2,192,1536,1]{3,2,4,1,0:T(8,128)(2,1)} %bitcast.74, bf16[64,1,8,1536]{3,2,1,0:T(8,128)(2,1)S(1)} %all-to-all-done), kind=kOutput, calls=%fused_computation.10 | convolution fusion | flops 2415919104 | bytes 9437184 | tf_op jit(solution)/shard_map/nscd,qsghd->nscgqh/dot_general | solution.py:77
  124.1 5.0 %convert_reduce_fusion = bf16[1536,64,8]{0,1,2:T(8,128)(2,1)} fusion(bf16[4,1,576,1536]{3,2,0,1:T(8,128)(2,1)} %bitcast.76, f32[64,1,8,2,4,192]{5,0,2,3,4,1:T(8,128)S(1)} %convolution_bitcast_fusion), kind=kOutput, calls=%fused_computation.5 | convolution fusion | flops 1214644224 | bytes 7077888 | tf_op jit(solution)/shard_map/nscqh,qshd->qnscd/dot_general | solution.py:81
  129.2 3.0 %reshape.436 = bf16[64,1,8,4,384]{4,3,0,2,1:T(4,128)(2,1)S(1)} reshape(bf16[64,8,1536]{2,0,1:T(8,128)(2,1)} %bitcast.77) | data formatting | bytes 3145728 | tf_op jit(solution)/shard_map/reshape | solution.py:86
  132.1 0.9 copy.45
  133.1 23.0 %all_to_all.30 = bf16[64,1,8,4,384]{4,2,0,1,3:T(8,128)(2,1)S(1)} all-to-all(bf16[64,1,8,4,384]{4,2,0,1,3:T(8,128)(2,1)S(1)} %copy.45), channel_id=1, replica_groups=mesh['wide'=64,'narrow'=4] {'narrow'}, dimensions={3} | all-to-all | bytes 3145728 | tf_op jit(solution)/shard_map/all_to_all | solution.py:87
  156.0 1.3 copy.66
  157.3 12.1 %all-to-all-start.2 = ((bf16[64,1,32,384]{3,2,1,0:T(8,128)(2,1)}), bf16[64,1,32,384]{3,2,1,0:T(8,128)(2,1)S(1)}, u32[]{:S(2)}, u32[]{:S(2)}) async-start(bf16[64,1,32,384]{3,2,1,0:T(8,128)(2,1)} %bitcast.73), calls=%async_computation.2 | async-start | bytes 3145728 | tf_op jit(solution)/shard_map/all_to_all | solution.py:89
  170.0 1.0 scatter_custom_fusion.2
  171.2 38.0 %all-to-all-done.2 = bf16[64,1,32,384]{3,2,1,0:T(8,128)(2,1)S(1)} async-done(((bf16[64,1,32,384]{3,2,1,0:T(8,128)(2,1)}), bf16[64,1,32,384]{3,2,1,0:T(8,128)(2,1)S(1)}, u32[]{:S(2)}, u32[]{:S(2)}) %all-to-all-start.2) | async-done | bytes 1572896 | tf_op jit(solution)/shard_map/all_to_all | solution.py:89
  209.2 1.9 gather_fusion
  211.3 0.5 multiply_reduce_fusion.2
  211.9 1.1 scatter_custom_fusion.1
  213.2 16.8 %all_to_all.31 = bf16[64,3,384]{2,1,0:T(4,128)(2,1)S(1)} all-to-all(bf16[64,3,384]{2,1,0:T(4,128)(2,1)S(1)} %fusion.12), channel_id=1, replica_groups=mesh['wide'=64,'narrow'=4] {'wide'}, dimensions={0} | all-to-all | bytes 294912 | tf_op jit(solution)/shard_map/all_to_all | solution.py:112
  230.4 1.6 scatter_custom_fusion.3
  (58 shorter events, 2.9 us)
Async XLA Ops:
  6.5 1.3 copy-start
  6.5 3.6 %copy-start.1 = (bf16[1,2,192,1536]{3,2,1,0:T(8,128)(2,1)S(1)}, bf16[1,2,192,1536]{3,2,1,0:T(8,128)(2,1)}, u32[]{:S(2)}) copy-start(bf16[1,2,192,1536]{3,2,1,0:T(8,128)(2,1)} %param.20) | copy-start | bytes 3538948
  6.5 3.6 %copy-start.2 = (bf16[1,192,1536]{2,1,0:T(8,128)(2,1)S(1)}, bf16[1,192,1536]{2,1,0:T(8,128)(2,1)}, u32[]{:S(2)}) copy-start(bf16[1,192,1536]{2,1,0:T(8,128)(2,1)} %param.21) | copy-start | bytes 1769476
  6.5 28.8 %reduce-scatter.4.cloned.1.call-start = ((), (), s32[]{:S(2)}) async-start(), calls=%async_computation.6 | async-start | bytes 491520
  10.1 103.9 %all-gather.3.cloned.1.call-start = ((), (), s32[]{:S(2)}) async-start(), calls=%async_computation.5 | async-start | bytes 8847360 | tf_op jit(solution)/shard_map/all_gather | solution.py:35
  11.6 0.7 copy-start.6
  11.6 0.9 copy-start.8
  11.6 1.1 copy-start.5
  11.6 24.8 %copy-start.3 = (bf16[128,384]{1,0:T(8,128)(2,1)S(1)}, bf16[128,384]{1,0:T(8,128)(2,1)}, u32[]{:S(2)}) copy-start(bf16[128,384]{1,0:T(8,128)(2,1)} %param.14) | copy-start | bytes 294916
  12.2 34.6 %copy-start.4 = (f32[1536]{0:T(1024)S(1)}, f32[1536]{0:T(1024)}, u32[]{:S(2)}) copy-start(f32[1536]{0:T(1024)} %param.15) | copy-start | bytes 18436
  54.0 64.9 %all-to-all-start = ((bf16[64,1,8,1536]{3,2,1,0:T(8,128)(2,1)}), bf16[64,1,8,1536]{3,2,1,0:T(8,128)(2,1)S(1)}, u32[]{:S(2)}, u32[]{:S(2)}) async-start(bf16[64,1,8,1536]{3,2,1,0:T(8,128)(2,1)} %bitcast.14), calls=%async_computation | async-start | bytes 3145728 | tf_op jit(solution)/shard_map/all_to_all | solution.py:76
  157.3 12.1 %copy-start.7 = (f32[128,4]{0,1:T(4,128)S(1)}, f32[128,4]{0,1:T(4,128)}, u32[]{:S(2)}) copy-start(f32[128,4]{0,1:T(4,128)} %param.17) | copy-start | bytes 6148
  157.3 51.8 %all-to-all-start.2 = ((bf16[64,1,32,384]{3,2,1,0:T(8,128)(2,1)}), bf16[64,1,32,384]{3,2,1,0:T(8,128)(2,1)S(1)}, u32[]{:S(2)}, u32[]{:S(2)}) async-start(bf16[64,1,32,384]{3,2,1,0:T(8,128)(2,1)} %bitcast.73), calls=%async_computation.2 | async-start | bytes 3145728 | tf_op jit(solution)/shard_map/all_to_all | solution.py:89
Sparse Core Ops, SparseCore 0:
  10.2 25.1 reduce-scatter.3
  37.2 76.7 all-gather.2
where the time goes:
time: 240 us; the launch traced here: 239 us
  waiting for transfers between devices  102 us (42%)
  blocking collectives  50 us (21%)
  starting transfers between devices  27.8 us (12%)
  local copies, waits for them, and re-layouts  26.9 us (11%)
  between operations  13.7 us (6%)
  matrix products  11.6 us (5%)
  other arithmetic  7.02 us (3%)
    all_gather x1, waiting for transfers between devices, local(): both = lax.all_gather(both, 'narrow', axis=0, tiled=False)  44.3 us
    all_to_all x1, waiting for transfers between devices, local(): lax.all_to_all(summed, 'wide', split_axis=0, concat_axis=0, tiled=True)  38 us
    all_to_all x1, blocking collectives, local(): lax.all_to_all(summed, 'narrow', split_axis=3, concat_axis=2, tiled=True)  23 us
    unnamed x3, waiting for transfers between devices  19.5 us
    all_to_all x1, blocking collectives, local(): lax.all_to_all(packed, 'wide', split_axis=0, concat_axis=0, tiled=True)  16.8 us
    all_to_all x1, starting transfers between devices, local(): lax.all_to_all(outgoing, 'wide', split_axis=0, concat_axis=0, tiled=True)  15.6 us
    all_to_all x1, starting transfers between devices, local(): lax.all_to_all(summed, 'wide', split_axis=0, concat_axis=0, tiled=True)  12.1 us
    all_gather x1, blocking collectives, local(): lax.all_gather(hidden, 'narrow', axis=1, tiled=True).astype(jnp.float32)  10.2 us
  transfers between devices with their start and end apart: 4, of which 3 were waited for; matrix products, arithmetic and copies ran while one was open for 8% of the time, Pallas kernels for 0%

commit v1 on v0

--- a/solution.py
+++ b/solution.py
@@ -1,3 +1,4 @@
+import functools
 import jax
 import jax.numpy as jnp
 from jax import lax
@@ -5,6 +6,16 @@
 
 EXPERTS = 32
 CAP = 32
+
+
+def settle_matrix_by_axis(my_data, group_axis):
+    parts_seen = []
+    for _ in range(lax.axis_size(group_axis)):
+        parts_seen.append(my_data)
+    return jnp.concatenate(lax.all_to_all(jnp.stack(parts_seen, 0), group_axis, 0, 0), 1)
+
+
+_number_keys = functools.partial(settle_matrix_by_axis, group_axis="narrow")
 
 
 def running_rank(onehot):
@@ -43,7 +54,7 @@
     ).astype(jnp.float32)
     hidden = (residual.astype(jnp.float32) + projected).astype(jnp.bfloat16)
     hidden_f = hidden.astype(jnp.float32)
-    whole_rows = lax.all_gather(hidden, "narrow", axis=1, tiled=True).astype(jnp.float32)
+    whole_rows = _number_keys(hidden).astype(jnp.float32)
     mean_sq = jnp.mean(whole_rows * whole_rows, axis=1, keepdims=True)
     normed = (whole_rows * lax.rsqrt(mean_sq + 1e-06) * norm_gain).astype(jnp.bfloat16)
     slot_count = slot_expert.shape[0]

time: 240 us -> 240 us (level)
  blocking collectives: 50 us -> 39.8 us
  waiting for transfers between devices: 102 us -> 109 us
    all_gather x1 -> x0, blocking collectives: 10.2 us -> none  [local(): lax.all_gather(hidden, 'narrow', axis=1, tiled=True).astype(jnp.float32)]
    all_to_all x0 -> x1, waiting for transfers between devices: none -> 6.15 us  [settle_matrix_by_axis(): lax.all_to_all(jnp.stack(parts_seen, 0), group_axis, 0, 0)]
    all_to_all x0 -> x1, starting transfers between devices: none -> 3.46 us  [settle_matrix_by_axis(): lax.all_to_all(jnp.stack(parts_seen, 0), group_axis, 0, 0)]
  transfers between devices with their start and end apart: 4 -> 5, of which waited for: 3 -> 4; matrix products, arithmetic and copies ran while one was open for 8% -> 9% of each run, Pallas kernels for 0% -> 0%
where the time goes in v1:
time: 240 us; the launch traced here: 239 us
  waiting for transfers between devices  109 us (45%)
  blocking collectives  39.8 us (17%)
  starting transfers between devices  29.7 us (12%)
  local copies, waits for them, and re-layouts  28.3 us (12%)
  between operations  13.8 us (6%)
  matrix products  11.6 us (5%)
  other arithmetic  7.18 us (3%)
    all_gather x1, waiting for transfers between devices, local(): both = lax.all_gather(both, 'narrow', axis=0, tiled=False)  44.8 us
    all_to_all x1, waiting for transfers between devices, local(): lax.all_to_all(summed, 'wide', split_axis=0, concat_axis=0, tiled=True)  38 us
    all_to_all x1, blocking collectives, local(): lax.all_to_all(summed, 'narrow', split_axis=3, concat_axis=2, tiled=True)  23 us
    unnamed x3, waiting for transfers between devices  19.6 us
    all_to_all x1, blocking collectives, local(): lax.all_to_all(packed, 'wide', split_axis=0, concat_axis=0, tiled=True)  16.8 us
    all_to_all x1, starting transfers between devices, local(): lax.all_to_all(outgoing, 'wide', split_axis=0, concat_axis=0, tiled=True)  14.1 us
    all_to_all x1, starting transfers between devices, local(): lax.all_to_all(summed, 'wide', split_axis=0, concat_axis=0, tiled=True)  12.1 us
    all_to_all x1, waiting for transfers between devices, settle_matrix_by_axis(): lax.all_to_all(jnp.stack(parts_seen, 0), group_axis, 0, 0)  6.15 us
  transfers between devices with their start and end apart: 5, of which 4 were waited for; matrix products, arithmetic and copies ran while one was open for 9% of the time, Pallas kernels for 0%

profile of v1, /device:TPU:1, one launch (start us, length us, event | category | flops | bytes accessed | tf_op | source)
XLA Modules:
  0.0 238.9 jit_solution(1588156797122013976)
XLA Ops:
  6.5 1.3 copy-done
  7.8 1.3 convolution_convert_fusion
  9.1 1.0 copy.69
  10.1 1.4 pad_maximum_fusion
  11.6 0.6 copy-done.6
  13.1 0.9 multiply_reduce_fusion.1
  14.2 1.2 reduce-window.6
  15.8 19.5 %reduce-scatter.4.cloned.1.call-done = bf16[384,128]{1,0:T(8,128)(2,1)} async-done(((bf16[1536,128]{1,0:T(8,128)(2,1)}), bf16[384,128]{1,0:T(8,128)(2,1)}) %reduce-scatter.4.cloned.1.call-update) | async-done | bytes 98320
  35.4 1.0 copy.70
  36.4 0.8 stack.2
  37.3 3.5 %all-to-all-start = ((bf16[4,128,384]{2,1,0:T(8,128)(2,1)}), bf16[4,128,384]{2,1,0:T(8,128)(2,1)S(1)}, u32[]{:S(2)}, u32[]{:S(2)}) async-start(bf16[4,128,384]{2,1,0:T(8,128)(2,1)} %stack.2), calls=%async_computation | async-start | bytes 786432 | tf_op jit(solution)/shard_map/all_to_all | solution.py:15
  40.8 6.1 %all-to-all-done = bf16[4,128,384]{2,1,0:T(8,128)(2,1)S(1)} async-done(((bf16[4,128,384]{2,1,0:T(8,128)(2,1)}), bf16[4,128,384]{2,1,0:T(8,128)(2,1)S(1)}, u32[]{:S(2)}, u32[]{:S(2)}) %all-to-all-start) | async-done | bytes 393248 | tf_op jit(solution)/shard_map/all_to_all | solution.py:15
  47.9 0.4 broadcast_in_dim.24
  48.3 1.4 reshape.409
  49.7 5.4 %scatter_custom_fusion = bf16[512,1536]{1,0:T(8,128)(2,1)} fusion(s32[512]{0:T(512)S(1)} %bitcast.93, bf16[512,1536]{1,0:T(8,128)(2,1)} %reshape.409, bf16[]{:T(256)} %constant.111.clone.1), kind=kCustom, calls=%fused_computation.25 | custom fusion | bytes 1573376 | tf_op jit(solution)/shard_map/scatter | solution.py:84
  55.0 14.1 %all-to-all-start.1 = ((bf16[64,1,8,1536]{3,2,1,0:T(8,128)(2,1)}), bf16[64,1,8,1536]{3,2,1,0:T(8,128)(2,1)S(1)}, u32[]{:S(2)}, u32[]{:S(2)}) async-start(bf16[64,1,8,1536]{3,2,1,0:T(8,128)(2,1)} %bitcast.16), calls=%async_computation.1 | async-start | bytes 3145728 | tf_op jit(solution)/shard_map/all_to_all | solution.py:87
  69.2 44.8 %all-gather.3.cloned.1.call-done = bf16[4,576,1536]{2,1,0:T(8,128)(2,1)} async-done(((bf16[1,576,1536]{2,1,0:T(8,128)(2,1)}), bf16[4,576,1536]{2,1,0:T(8,128)(2,1)}) %all-gather.3.cloned.1.call-update) | async-done | bytes 7077904 | tf_op jit(solution)/shard_map/all_gather | solution.py:46
  114.0 4.9 %slice.58 = bf16[4,1,384,1536]{3,2,0,1:T(8,128)(2,1)} slice(bf16[4,1,576,1536]{3,2,0,1:T(8,128)(2,1)} %bitcast.83), slice={[0:4], [0:1], [0:384], [0:1536]} | slice | bytes 9437184 | tf_op jit(solution)/shard_map/slice | solution.py:47
  118.8 5.3 %convolution_bitcast_fusion = f32[64,1,8,2,4,192]{5,0,2,3,4,1:T(8,128)S(1)} fusion(bf16[4,2,192,1536,1]{3,2,4,1,0:T(8,128)(2,1)} %bitcast.82, bf16[64,1,8,1536]{3,2,1,0:T(8,128)(2,1)S(1)} %all-to-all-done.1), kind=kOutput, calls=%fused_computation.10 | convolution fusion | flops 2415919104 | bytes 9437184 | tf_op jit(solution)/shard_map/nscd,qsghd->nscgqh/dot_general | solution.py:88
  124.2 5.0 %convert_reduce_fusion = bf16[1536,64,8]{0,1,2:T(8,128)(2,1)} fusion(bf16[4,1,576,1536]{3,2,0,1:T(8,128)(2,1)} %bitcast.84, f32[64,1,8,2,4,192]{5,0,2,3,4,1:T(8,128)S(1)} %convolution_bitcast_fusion), kind=kOutput, calls=%fused_computation.5 | convolution fusion | flops 1214644224 | bytes 7077888 | tf_op jit(solution)/shard_map/nscqh,qshd->qnscd/dot_general | solution.py:92
  129.2 3.0 %reshape.443 = bf16[64,1,8,4,384]{4,3,0,2,1:T(4,128)(2,1)S(1)} reshape(bf16[64,8,1536]{2,0,1:T(8,128)(2,1)} %bitcast.85) | data formatting | bytes 3145728 | tf_op jit(solution)/shard_map/reshape | solution.py:97
  132.2 0.9 copy.60
  133.1 23.0 %all_to_all.35 = bf16[64,1,8,4,384]{4,2,0,1,3:T(8,128)(2,1)S(1)} all-to-all(bf16[64,1,8,4,384]{4,2,0,1,3:T(8,128)(2,1)S(1)} %copy.60), channel_id=1, replica_groups=mesh['wide'=64,'narrow'=4] {'narrow'}, dimensions={3} | all-to-all | bytes 3145728 | tf_op jit(solution)/shard_map/all_to_all | solution.py:98
  156.1 1.3 copy.81
  157.4 12.1 %all-to-all-start.3 = ((bf16[64,1,32,384]{3,2,1,0:T(8,128)(2,1)}), bf16[64,1,32,384]{3,2,1,0:T(8,128)(2,1)S(1)}, u32[]{:S(2)}, u32[]{:S(2)}) async-start(bf16[64,1,32,384]{3,2,1,0:T(8,128)(2,1)} %bitcast.81), calls=%async_computation.3 | async-start | bytes 3145728 | tf_op jit(solution)/shard_map/all_to_all | solution.py:100
  170.1 1.0 scatter_custom_fusion.2
  171.2 38.0 %all-to-all-done.3 = bf16[64,1,32,384]{3,2,1,0:T(8,128)(2,1)S(1)} async-done(((bf16[64,1,32,384]{3,2,1,0:T(8,128)(2,1)}), bf16[64,1,32,384]{3,2,1,0:T(8,128)(2,1)S(1)}, u32[]{:S(2)}, u32[]{:S(2)}) %all-to-all-start.3) | async-done | bytes 1572896 | tf_op jit(solution)/shard_map/all_to_all | solution.py:100
  209.2 1.9 gather_fusion
  211.4 0.5 multiply_reduce_fusion.2
  211.9 1.1 scatter_custom_fusion.1
  213.2 16.8 %all_to_all.36 = bf16[64,3,384]{2,1,0:T(4,128)(2,1)S(1)} all-to-all(bf16[64,3,384]{2,1,0:T(4,128)(2,1)S(1)} %fusion.11), channel_id=1, replica_groups=mesh['wide'=64,'narrow'=4] {'wide'}, dimensions={0} | all-to-all | bytes 294912 | tf_op jit(solution)/shard_map/all_to_all | solution.py:123
  230.4 1.6 scatter_custom_fusion.3
  (62 shorter events, 4.0 us)
Async XLA Ops:
  6.5 1.3 copy-start
  6.5 3.6 %copy-start.1 = (bf16[1,2,192,1536]{3,2,1,0:T(8,128)(2,1)S(1)}, bf16[1,2,192,1536]{3,2,1,0:T(8,128)(2,1)}, u32[]{:S(2)}) copy-start(bf16[1,2,192,1536]{3,2,1,0:T(8,128)(2,1)} %param.20) | copy-start | bytes 3538948
  6.5 3.6 %copy-start.2 = (bf16[1,192,1536]{2,1,0:T(8,128)(2,1)S(1)}, bf16[1,192,1536]{2,1,0:T(8,128)(2,1)}, u32[]{:S(2)}) copy-start(bf16[1,192,1536]{2,1,0:T(8,128)(2,1)} %param.21) | copy-start | bytes 1769476
  6.5 28.8 %reduce-scatter.4.cloned.1.call-start = ((), (), s32[]{:S(2)}) async-start(), calls=%async_computation.7 | async-start | bytes 491520
  10.1 103.9 %all-gather.3.cloned.1.call-start = ((), (), s32[]{:S(2)}) async-start(), calls=%async_computation.6 | async-start | bytes 8847360 | tf_op jit(solution)/shard_map/all_gather | solution.py:46
  11.6 0.7 copy-start.6
  11.6 0.9 copy-start.8
  11.6 1.1 copy-start.5
  11.6 24.8 %copy-start.3 = (bf16[128,384]{1,0:T(8,128)(2,1)S(1)}, bf16[128,384]{1,0:T(8,128)(2,1)}, u32[]{:S(2)}) copy-start(bf16[128,384]{1,0:T(8,128)(2,1)} %param.14) | copy-start | bytes 294916
  14.2 33.2 %copy-start.4 = (f32[1536]{0:T(1024)S(1)}, f32[1536]{0:T(1024)}, u32[]{:S(2)}) copy-start(f32[1536]{0:T(1024)} %param.15) | copy-start | bytes 18436
  37.3 9.7 %all-to-all-start = ((bf16[4,128,384]{2,1,0:T(8,128)(2,1)}), bf16[4,128,384]{2,1,0:T(8,128)(2,1)S(1)}, u32[]{:S(2)}, u32[]{:S(2)}) async-start(bf16[4,128,384]{2,1,0:T(8,128)(2,1)} %stack.2), calls=%async_computation | async-start | bytes 786432 | tf_op jit(solution)/shard_map/all_to_all | solution.py:15
  55.0 63.8 %all-to-all-start.1 = ((bf16[64,1,8,1536]{3,2,1,0:T(8,128)(2,1)}), bf16[64,1,8,1536]{3,2,1,0:T(8,128)(2,1)S(1)}, u32[]{:S(2)}, u32[]{:S(2)}) async-start(bf16[64,1,8,1536]{3,2,1,0:T(8,128)(2,1)} %bitcast.16), calls=%async_computation.1 | async-start | bytes 3145728 | tf_op jit(solution)/shard_map/all_to_all | solution.py:87
  157.4 12.1 %copy-start.7 = (f32[128,4]{0,1:T(4,128)S(1)}, f32[128,4]{0,1:T(4,128)}, u32[]{:S(2)}) copy-start(f32[128,4]{0,1:T(4,128)} %param.17) | copy-start | bytes 6148
  157.4 51.9 %all-to-all-start.3 = ((bf16[64,1,32,384]{3,2,1,0:T(8,128)(2,1)}), bf16[64,1,32,384]{3,2,1,0:T(8,128)(2,1)S(1)}, u32[]{:S(2)}, u32[]{:S(2)}) async-start(bf16[64,1,32,384]{3,2,1,0:T(8,128)(2,1)} %bitcast.81), calls=%async_computation.3 | async-start | bytes 3145728 | tf_op jit(solution)/shard_map/all_to_all | solution.py:100
Sparse Core Ops, SparseCore 0:
  10.2 25.1 reduce-scatter.3
  37.2 76.7 all-gather.2
